TPU v7x, 128 devices: a whole 4x4x4 slice. The times are simulated.
128 devices in a mesh: section: 16 (over x, z_hi, core), expert: 8 (over z_lo, y).
Axes of the slice: x: 4, y: 4, z: 4 (z_hi: 2, z_lo: 2; z = z_hi * 2 + z_lo), core: 2. Of those that a mesh axis runs over, the one named last changes fastest.
Arguments:
- grad_in: bfloat16 [16, 1024, 4096], P('section', 'expert'), may hold values from -6 to 6
- saved_inputs: bfloat16 [3, 16, 1024, 4096], P(None, 'section', 'expert'), may hold values from -6 to 6
- expert_ids: int32 [3, 16, 1024, 2], P(None, 'section', 'expert'), may hold values from 0 to 7, as said below
- slots: int32 [3, 16, 1024, 2], P(None, 'section', 'expert'), may hold values from 0 to 36, as said below
- gates: float32 [3, 16, 1024, 2], P(None, 'section', 'expert'), may hold values from 0.05 to 0.8
- w_gate: bfloat16 [16, 8, 4096, 768], P('section', 'expert'), may hold values from -0.09375 to 0.09375
- w_up: bfloat16 [16, 8, 4096, 768], P('section', 'expert'), may hold values from -0.09375 to 0.09375
- w_down: bfloat16 [16, 8, 768, 4096], P('section', 'expert'), may hold values from -0.21875 to 0.21875
Outputs:
- grad_out: bfloat16 [16, 1024, 4096], P('section', 'expert')
Inputs may be any that keep to these rules, and one draw needn't show every extreme that they name: `expert_ids`: each token names 2 different experts; every expert is named. `slots`: among the routes of the tokens of one device (aligned blocks of 128 tokens) to one expert, taken in some order, the n-th has slot min(n, 36) for n = 0, 1, ...; in every round and section some such group has more than 36 routes.
All inputs are finite; a program needn't handle non-finite values.
Results may differ from a plain program's by a relative error of at most 0.0075.
Values may be sent and summed in bfloat16 or wider, within the bound.
No kernel may reach another device: no remote copies, remote signals or barrier semaphores. Data moves between devices by JAX's collectives and lax.ppermute only.
A program may use at most 128 MiB of HBM per device.

v0:
```python
import jax
import jax.numpy as jnp
from jax import lax
from jax.sharding import PartitionSpec as P


def shifted(x, axis, by):
    devices = lax.axis_size(axis)
    return lax.ppermute(x, axis, [(i, (i + by) % devices) for i in range(devices)])


def forward_part(input_part, gate_proj, up_proj):
    pre_gate = jnp.einsum("scjl,jlh->sch", input_part, gate_proj, preferred_element_type=jnp.float32)
    pre_up = jnp.einsum("scjl,jlh->sch", input_part, up_proj, preferred_element_type=jnp.float32)
    return pre_gate, pre_up


def backward_part(grad_part, pre_gate, pre_up, gate_proj, up_proj, down_proj):
    grad_hidden = jnp.einsum("scjl,hjl->sch", grad_part, down_proj, preferred_element_type=jnp.float32)
    sigma = jax.nn.sigmoid(pre_gate)
    derivative = sigma * (1.0 + pre_gate * (1.0 - sigma))
    grad_gate = (grad_hidden * pre_up * derivative).astype(jnp.bfloat16)
    grad_up = (grad_hidden * pre_gate * sigma).astype(jnp.bfloat16)
    summed = jnp.einsum("sch,jlh->scjl", grad_gate, gate_proj, preferred_element_type=jnp.float32)
    summed = summed + jnp.einsum("sch,jlh->scjl", grad_up, up_proj, preferred_element_type=jnp.float32)
    return summed.astype(jnp.bfloat16)


def per_device(grad_in, saved_inputs, expert_ids, slots, gates, w_gate, w_up, w_down):
    groups = lax.axis_size("expert")
    rows_dev = grad_in.shape[1]
    width = grad_in.shape[2]
    rounds = saved_inputs.shape[0]
    capacity = 9 * rows_dev * expert_ids.shape[-1] // (8 * groups)
    lanes = 128
    pieces = width // lanes
    columns = groups * capacity
    hidden = w_gate.shape[-1]
    gate_proj = w_gate[0, 0].reshape(pieces, lanes, hidden)
    up_proj = w_up[0, 0].reshape(pieces, lanes, hidden)
    down_proj = w_down[0, 0].reshape(hidden, pieces, lanes)
    column_ids = jnp.arange(columns, dtype=jnp.int32)

    def route_plan(step):
        route_ids = expert_ids[step, 0]
        slot_ids = slots[step, 0]
        target = jnp.where(slot_ids < capacity, route_ids * capacity + slot_ids, -1)
        hit = target[:, :, None] == column_ids[None, None, :]
        dispatch = jnp.any(hit, axis=1).T.astype(jnp.bfloat16).reshape(groups, capacity, rows_dev)
        weights = jnp.sum(jnp.where(hit, gates[step, 0][:, :, None], 0.0), axis=1)
        weights_hi = weights.astype(jnp.bfloat16)
        weights_lo = (weights - weights_hi.astype(jnp.float32)).astype(jnp.bfloat16)
        shape = (rows_dev, groups, capacity)
        return dispatch, weights_hi.reshape(shape), weights_lo.reshape(shape)

    def collect(dispatch, rows):
        picked = jnp.einsum("ect,tjl->ecjl", dispatch, rows, preferred_element_type=jnp.float32)
        return picked.astype(jnp.bfloat16)

    def exchange(buffer):
        count = buffer.shape[1]
        flat = buffer.reshape(groups, count * pieces, lanes)
        moved = lax.all_to_all(flat, "expert", split_axis=0, concat_axis=0, tiled=True)
        return moved.reshape(groups, count, pieces, lanes)

    plans = [route_plan(step) for step in range(rounds)]
    first_part = exchange(collect(plans[0][0], saved_inputs[0, 0].reshape(rows_dev, pieces, lanes)))
    first_part, first_block, later_inputs, down_raw = lax.optimization_barrier(
        (first_part, grad_in[0], saved_inputs[1:], w_down[0, 0])
    )
    down_proj = down_raw.reshape(hidden, pieces, lanes)
    input_buffers = [None] + [
        collect(plans[step][0], later_inputs[step - 1, 0].reshape(rows_dev, pieces, lanes))
        for step in range(1, rounds)
    ]
    pre_gate, pre_up = forward_part(first_part, gate_proj, up_proj)
    bounds = [(0, capacity // 2), (capacity // 2, capacity)]

    present_block = first_block.reshape(rows_dev, pieces, lanes)
    for step in range(rounds):
        dispatch, weights_hi, weights_lo = plans[step]
        if step > 0:
            next_part, present_block = lax.optimization_barrier((next_part, present_block))
        grad_parts = [exchange(collect(dispatch[:, lo:hi], present_block)) for lo, hi in bounds]
        if step > 0:
            pre_gate, pre_up = forward_part(next_part, gate_proj, up_proj)
        results = [
            backward_part(grad_parts[i], pre_gate[:, lo:hi], pre_up[:, lo:hi], gate_proj, up_proj, down_proj)
            for i, (lo, hi) in enumerate(bounds)
        ]
        summed = present_block.astype(jnp.float32)
        for i, (lo, hi) in enumerate(bounds):
            arrived = exchange(results[i])
            if i + 1 == len(bounds) and step + 1 < rounds:
                arrived, next_buffer = lax.optimization_barrier((arrived, input_buffers[step + 1]))
                next_part = exchange(next_buffer)
            summed = summed + jnp.einsum(
                "tec,ecjl->tjl", weights_hi[:, :, lo:hi], arrived, preferred_element_type=jnp.float32
            )
            summed = summed + jnp.einsum(
                "tec,ecjl->tjl", weights_lo[:, :, lo:hi], arrived, preferred_element_type=jnp.float32
            )
        present_block = shifted(summed.astype(jnp.bfloat16), "section", -1)
    return present_block.reshape(1, rows_dev, width)


def solution(mesh):
    placed = (
        P("section", "expert", None),
        P(None, "section", "expert", None),
        P(None, "section", "expert", None),
        P(None, "section", "expert", None),
        P(None, "section", "expert", None),
        P("section", "expert", None, None),
        P("section", "expert", None, None),
        P("section", "expert", None, None),
    )
    return jax.shard_map(
        per_device,
        mesh=mesh,
        in_specs=placed,
        out_specs=P("section", "expert", None),
        check_vma=False,
    )
```

profile of v0, /device:TPU:7, one launch (start us, length us, event | category | flops | bytes accessed | tf_op | source)
XLA Modules:
  0.0 420.3 jit_solution(12487506966541314835)
XLA Ops:
  5.3 5.5 %all-to-all-start = ((bf16[8,1152,128]{2,1,0:T(8,128)(2,1)}), bf16[8,1152,128]{2,1,0:T(8,128)(2,1)}, u32[]{:S(2)}, u32[]{:S(2)}) async-start(bf16[8,1152,128]{2,1,0:T(8,128)(2,1)} %bitcast.11), calls=%async_computation | async-start | bytes 4718592 | tf_op jit(solution)/shard_map/all_to_all | solution.py:63
  17.2 23.6 %all-to-all-done = bf16[8,1152,128]{2,1,0:T(8,128)(2,1)} async-done(((bf16[8,1152,128]{2,1,0:T(8,128)(2,1)}), bf16[8,1152,128]{2,1,0:T(8,128)(2,1)}, u32[]{:S(2)}, u32[]{:S(2)}) %all-to-all-start) | async-done | bytes 2359328 | tf_op jit(solution)/shard_map/all_to_all | solution.py:63
  43.3 6.1 %all-to-all-start.1 = ((bf16[8,576,128]{2,1,0:T(8,128)(2,1)}), bf16[8,576,128]{2,1,0:T(8,128)(2,1)}, u32[]{:S(2)}, u32[]{:S(2)}) async-start(bf16[8,576,128]{2,1,0:T(8,128)(2,1)} %bitcast.442), calls=%async_computation.1 | async-start | bytes 2359296 | tf_op jit(solution)/shard_map/all_to_all | solution.py:63
  50.7 7.5 %fusion.54 = f32[8,36,768]{2,1,0:T(8,128)} fusion(bf16[32,128,768,1]{2,1,0,3:T(8,128)(2,1)} %bitcast.401, bf16[8,36,32,128]{3,2,1,0:T(8,128)(2,1)} %bitcast.12), kind=kOutput, calls=%fused_computation.82 | convolution fusion | flops 1811939328 | bytes 9535488 | tf_op jit(solution)/shard_map/scjl,jlh->sch/dot_general | solution.py:14
  58.2 4.3 %fusion.57 = f32[8,36,768]{2,1,0:T(8,128)S(1)} fusion(bf16[32,128,768,1]{2,1,0,3:T(8,128)(2,1)S(1)} %bitcast.474, bf16[8,36,32,128]{3,2,1,0:T(8,128)(2,1)} %bitcast.12), kind=kOutput, calls=%fused_computation.83 | convolution fusion | flops 1811939328 | bytes 9535488 | tf_op jit(solution)/shard_map/scjl,jlh->sch/dot_general | solution.py:13
  62.5 4.2 all-to-all-done.1
  70.5 5.6 %fusion.72 = f32[8,18,768]{2,1,0:T(8,128)S(1)} fusion(bf16[8,18,32,128]{3,2,1,0:T(8,128)(2,1)} %bitcast.18, bf16[768,4096]{1,0:T(8,128)(2,1)} %bitcast.458), kind=kOutput, calls=%fused_computation.88 | convolution fusion | flops 905969664 | bytes 7913472 | tf_op jit(solution)/shard_map/scjl,hjl->sch/dot_general | solution.py:19
  76.1 4.6 %fusion.122 = f32[8,18,32,128]{3,1,2,0:T(8,128)S(1)} fusion(bf16[32,128,768,1]{2,1,0,3:T(8,128)(2,1)} %bitcast.464, f32[8,18,768]{2,1,0:T(8,128)S(1)} %fusion.72, f32[8,36,768]{2,1,0:T(8,128)S(1)} %copy-done.24, f32[8,36,768]{2,1,0:T(8,128)S(1)} %fusion.57), kind=kOutput, calls=%fused_computation.144 | convolution fusion | flops 907075584 | bytes 10420224 | tf_op jit(solution)/shard_map/sch,jlh->scjl/dot_general | solution.py:24
  92.3 5.6 %fusion.75 = f32[8,18,768]{2,1,0:T(8,128)S(1)} fusion(bf16[8,18,32,128]{3,2,1,0:T(8,128)(2,1)} %bitcast.449, bf16[768,4096]{1,0:T(8,128)(2,1)} %bitcast.459), kind=kOutput, calls=%fused_computation.89 | convolution fusion | flops 905969664 | bytes 7913472 | tf_op jit(solution)/shard_map/scjl,hjl->sch/dot_general | solution.py:19
  97.9 4.5 %fusion.119 = f32[8,18,32,128]{3,1,2,0:T(8,128)S(1)} fusion(bf16[32,128,768,1]{2,1,0,3:T(8,128)(2,1)} %bitcast.465, f32[8,18,768]{2,1,0:T(8,128)S(1)} %fusion.75, f32[8,36,768]{2,1,0:T(8,128)S(1)} %copy-done.25, f32[8,36,768]{2,1,0:T(8,128)S(1)} %fusion.57), kind=kOutput, calls=%fused_computation.141 | convolution fusion | flops 907075584 | bytes 10420224 | tf_op jit(solution)/shard_map/sch,jlh->scjl/dot_general | solution.py:24
  123.3 6.9 %all-to-all-done.5 = bf16[8,576,128]{2,1,0:T(8,128)(2,1)S(1)} async-done(((bf16[8,576,128]{2,1,0:T(8,128)(2,1)}), bf16[8,576,128]{2,1,0:T(8,128)(2,1)S(1)}, u32[]{:S(2)}, u32[]{:S(2)}) %all-to-all-start.5) | async-done | bytes 1179680 | tf_op jit(solution)/shard_map/all_to_all | solution.py:63
  130.2 4.8 %all-to-all-start.3 = ((bf16[8,1152,128]{2,1,0:T(8,128)(2,1)}), bf16[8,1152,128]{2,1,0:T(8,128)(2,1)}, u32[]{:S(2)}, u32[]{:S(2)}) async-start(bf16[8,1152,128]{2,1,0:T(8,128)(2,1)} %bitcast.437), calls=%async_computation.3 | async-start | bytes 4718592 | tf_op jit(solution)/shard_map/all_to_all | solution.py:63
  139.4 36.6 %collective-permute-done = bf16[128,32,128]{2,0,1:T(8,128)(2,1)S(1)} collective-permute-done((bf16[128,32,128]{2,0,1:T(8,128)(2,1)S(1)}, bf16[128,32,128]{2,0,1:T(8,128)(2,1)S(1)}, u32[]{:S(2)}, u32[]{:S(2)}) %collective-permute-start) | collective-permute-done | bytes 1048608 | tf_op jit(solution)/shard_map/ppermute | solution.py:9
  178.4 4.4 %all-to-all-start.6 = ((bf16[8,576,128]{2,1,0:T(8,128)(2,1)}), bf16[8,576,128]{2,1,0:T(8,128)(2,1)}, u32[]{:S(2)}, u32[]{:S(2)}) async-start(bf16[8,576,128]{2,1,0:T(8,128)(2,1)} %bitcast.443), calls=%async_computation.6 | async-start | bytes 2359296 | tf_op jit(solution)/shard_map/all_to_all | solution.py:63
  182.8 7.1 %fusion.60 = f32[8,36,768]{2,1,0:T(8,128)} fusion(bf16[32,128,768,1]{2,1,0,3:T(8,128)(2,1)} %bitcast.402, bf16[8,36,32,128]{3,2,1,0:T(8,128)(2,1)} %bitcast.41), kind=kOutput, calls=%fused_computation.84 | convolution fusion | flops 1811939328 | bytes 9535488 | tf_op jit(solution)/shard_map/scjl,jlh->sch/dot_general | solution.py:14
  191.2 5.9 %fusion.63 = f32[8,36,768]{2,1,0:T(8,128)S(1)} fusion(bf16[32,128,768,1]{2,1,0,3:T(8,128)(2,1)} %bitcast.466, bf16[8,36,32,128]{3,2,1,0:T(8,128)(2,1)} %bitcast.41), kind=kOutput, calls=%fused_computation.85 | convolution fusion | flops 1811939328 | bytes 9535488 | tf_op jit(solution)/shard_map/scjl,jlh->sch/dot_general | solution.py:13
  204.0 5.6 %fusion.78 = f32[8,18,768]{2,1,0:T(8,128)S(1)} fusion(bf16[8,18,32,128]{3,2,1,0:T(8,128)(2,1)} %bitcast.72, bf16[768,4096]{1,0:T(8,128)(2,1)} %bitcast.460), kind=kOutput, calls=%fused_computation.90 | convolution fusion | flops 905969664 | bytes 7913472 | tf_op jit(solution)/shard_map/scjl,hjl->sch/dot_general | solution.py:19
  209.6 4.6 %fusion.116 = f32[8,18,32,128]{3,1,2,0:T(8,128)S(1)} fusion(bf16[32,128,768,1]{2,1,0,3:T(8,128)(2,1)} %bitcast.467, f32[8,18,768]{2,1,0:T(8,128)S(1)} %fusion.78, f32[8,36,768]{2,1,0:T(8,128)S(1)} %copy-done.20, f32[8,36,768]{2,1,0:T(8,128)S(1)} %fusion.63), kind=kOutput, calls=%fused_computation.138 | convolution fusion | flops 907075584 | bytes 10420224 | tf_op jit(solution)/shard_map/sch,jlh->scjl/dot_general | solution.py:24
  225.8 5.6 %fusion.81 = f32[8,18,768]{2,1,0:T(8,128)S(1)} fusion(bf16[8,18,32,128]{3,2,1,0:T(8,128)(2,1)} %bitcast.450, bf16[768,4096]{1,0:T(8,128)(2,1)} %bitcast.461), kind=kOutput, calls=%fused_computation.91 | convolution fusion | flops 905969664 | bytes 7913472 | tf_op jit(solution)/shard_map/scjl,hjl->sch/dot_general | solution.py:19
  231.4 4.5 %fusion.113 = f32[8,18,32,128]{3,1,2,0:T(8,128)S(1)} fusion(bf16[32,128,768,1]{2,1,0,3:T(8,128)(2,1)} %bitcast.468, f32[8,18,768]{2,1,0:T(8,128)S(1)} %fusion.81, f32[8,36,768]{2,1,0:T(8,128)S(1)} %copy-done.21, f32[8,36,768]{2,1,0:T(8,128)S(1)} %fusion.63), kind=kOutput, calls=%fused_computation.135 | convolution fusion | flops 907075584 | bytes 10420224 | tf_op jit(solution)/shard_map/sch,jlh->scjl/dot_general | solution.py:24
  257.8 5.9 %all-to-all-done.10 = bf16[8,576,128]{2,1,0:T(8,128)(2,1)S(1)} async-done(((bf16[8,576,128]{2,1,0:T(8,128)(2,1)}), bf16[8,576,128]{2,1,0:T(8,128)(2,1)S(1)}, u32[]{:S(2)}, u32[]{:S(2)}) %all-to-all-start.10) | async-done | bytes 1179680 | tf_op jit(solution)/shard_map/all_to_all | solution.py:63
  263.7 4.6 %all-to-all-start.8 = ((bf16[8,1152,128]{2,1,0:T(8,128)(2,1)}), bf16[8,1152,128]{2,1,0:T(8,128)(2,1)}, u32[]{:S(2)}, u32[]{:S(2)}) async-start(bf16[8,1152,128]{2,1,0:T(8,128)(2,1)} %bitcast.438), calls=%async_computation.8 | async-start | bytes 4718592 | tf_op jit(solution)/shard_map/all_to_all | solution.py:63
  273.3 33.0 %collective-permute-done.1 = bf16[128,32,128]{2,0,1:T(8,128)(2,1)S(1)} collective-permute-done((bf16[128,32,128]{2,0,1:T(8,128)(2,1)S(1)}, bf16[128,32,128]{2,0,1:T(8,128)(2,1)S(1)}, u32[]{:S(2)}, u32[]{:S(2)}) %collective-permute-start.1) | collective-permute-done | bytes 1048608 | tf_op jit(solution)/shard_map/ppermute | solution.py:9
  309.0 8.3 %all-to-all-start.13 = ((bf16[8,576,128]{2,1,0:T(8,128)(2,1)}), bf16[8,576,128]{2,1,0:T(8,128)(2,1)}, u32[]{:S(2)}, u32[]{:S(2)}) async-start(bf16[8,576,128]{2,1,0:T(8,128)(2,1)} %bitcast.444), calls=%async_computation.13 | async-start | bytes 2359296 | tf_op jit(solution)/shard_map/all_to_all | solution.py:63
  317.3 7.1 %fusion.66 = f32[8,36,768]{2,1,0:T(8,128)} fusion(bf16[32,128,768,1]{2,1,0,3:T(8,128)(2,1)} %bitcast.403, bf16[8,36,32,128]{3,2,1,0:T(8,128)(2,1)} %bitcast.92), kind=kOutput, calls=%fused_computation.86 | convolution fusion | flops 1811939328 | bytes 9535488 | tf_op jit(solution)/shard_map/scjl,jlh->sch/dot_general | solution.py:14
  325.6 5.8 %fusion.69 = f32[8,36,768]{2,1,0:T(8,128)S(1)} fusion(bf16[32,128,768,1]{2,1,0,3:T(8,128)(2,1)} %bitcast.469, bf16[8,36,32,128]{3,2,1,0:T(8,128)(2,1)} %bitcast.92), kind=kOutput, calls=%fused_computation.87 | convolution fusion | flops 1811939328 | bytes 9535488 | tf_op jit(solution)/shard_map/scjl,jlh->sch/dot_general | solution.py:13
  338.4 5.6 %fusion.87 = f32[8,18,768]{2,1,0:T(8,128)S(1)} fusion(bf16[8,18,32,128]{3,2,1,0:T(8,128)(2,1)} %bitcast.148, bf16[768,4096]{1,0:T(8,128)(2,1)} %bitcast.462), kind=kOutput, calls=%fused_computation.93 | convolution fusion | flops 905969664 | bytes 7913472 | tf_op jit(solution)/shard_map/scjl,hjl->sch/dot_general | solution.py:19
  344.0 4.6 %fusion.107 = f32[8,18,32,128]{3,1,2,0:T(8,128)S(1)} fusion(bf16[32,128,768,1]{2,1,0,3:T(8,128)(2,1)} %bitcast.470, f32[8,18,768]{2,1,0:T(8,128)S(1)} %fusion.87, f32[8,36,768]{2,1,0:T(8,128)S(1)} %copy-done.22, f32[8,36,768]{2,1,0:T(8,128)S(1)} %fusion.69), kind=kOutput, calls=%fused_computation.129 | convolution fusion | flops 907075584 | bytes 10420224 | tf_op jit(solution)/shard_map/sch,jlh->scjl/dot_general | solution.py:24
  360.2 5.6 %fusion.84 = f32[8,18,768]{2,1,0:T(8,128)S(1)} fusion(bf16[8,18,32,128]{3,2,1,0:T(8,128)(2,1)} %bitcast.451, bf16[768,4096]{1,0:T(8,128)(2,1)} %bitcast.463), kind=kOutput, calls=%fused_computation.92 | convolution fusion | flops 905969664 | bytes 7913472 | tf_op jit(solution)/shard_map/scjl,hjl->sch/dot_general | solution.py:19
  365.8 4.5 %fusion.110 = f32[8,18,32,128]{3,1,2,0:T(8,128)S(1)} fusion(bf16[32,128,768,1]{2,1,0,3:T(8,128)(2,1)} %bitcast.471, f32[8,18,768]{2,1,0:T(8,128)S(1)} %fusion.84, f32[8,36,768]{2,1,0:T(8,128)S(1)} %copy-done.23, f32[8,36,768]{2,1,0:T(8,128)S(1)} %fusion.69), kind=kOutput, calls=%fused_computation.132 | convolution fusion | flops 907075584 | bytes 10420224 | tf_op jit(solution)/shard_map/sch,jlh->scjl/dot_general | solution.py:24
  385.1 13.0 %all-to-all-done.12 = bf16[8,576,128]{2,1,0:T(8,128)(2,1)S(1)} async-done(((bf16[8,576,128]{2,1,0:T(8,128)(2,1)}), bf16[8,576,128]{2,1,0:T(8,128)(2,1)S(1)}, u32[]{:S(2)}, u32[]{:S(2)}) %all-to-all-start.12) | async-done | bytes 1179680 | tf_op jit(solution)/shard_map/all_to_all | solution.py:63
  403.0 14.9 %collective-permute-done.2 = bf16[128,32,128]{2,0,1:T(8,128)(2,1)S(1)} collective-permute-done((bf16[128,32,128]{2,0,1:T(8,128)(2,1)S(1)}, bf16[128,32,128]{2,0,1:T(8,128)(2,1)S(1)}, u32[]{:S(2)}, u32[]{:S(2)}) %collective-permute-start.2) | collective-permute-done | bytes 1048608 | tf_op jit(solution)/shard_map/ppermute | solution.py:9
  (180 shorter events, 148.8 us)
Async XLA Ops:
  1.9 13.3 %copy-start.16 = (s32[128,2]{0,1:T(2,128)}, s32[128,2]{0,1:T(2,128)S(1)}, u32[]{:S(2)}) copy-start(s32[128,2]{0,1:T(2,128)S(1)} %get-tuple-element.38) | copy-start | bytes 3076
  2.0 244.5 %copy-start.11 = (pred[128,288]{0,1:T(8,128)(4,1)}, pred[128,288]{0,1:T(8,128)(4,1)S(1)}, u32[]{:S(2)}) copy-start(pred[128,288]{0,1:T(8,128)(4,1)S(1)} %get-tuple-element.45) | copy-start | bytes 110596
  5.3 35.5 %all-to-all-start = ((bf16[8,1152,128]{2,1,0:T(8,128)(2,1)}), bf16[8,1152,128]{2,1,0:T(8,128)(2,1)}, u32[]{:S(2)}, u32[]{:S(2)}) async-start(bf16[8,1152,128]{2,1,0:T(8,128)(2,1)} %bitcast.11), calls=%async_computation | async-start | bytes 4718592 | tf_op jit(solution)/shard_map/all_to_all | solution.py:63
  43.3 23.4 %all-to-all-start.1 = ((bf16[8,576,128]{2,1,0:T(8,128)(2,1)}), bf16[8,576,128]{2,1,0:T(8,128)(2,1)}, u32[]{:S(2)}, u32[]{:S(2)}) async-start(bf16[8,576,128]{2,1,0:T(8,128)(2,1)} %bitcast.442), calls=%async_computation.1 | async-start | bytes 2359296 | tf_op jit(solution)/shard_map/all_to_all | solution.py:63
  49.4 8.8 %slice-start.14 = ((s8[6291456]{0:T(1024)(128)(4,1)}), s8[4194304]{0:T(1024)(128)(4,1)S(1)}, s32[]{:S(2)}) async-start(s8[6291456]{0:T(1024)(128)(4,1)} %bitcast.472), calls=%async_computation.29 | async-start | bytes 8388608
  50.7 7.5 %slice-start.15 = ((s8[6291456]{0:T(1024)(128)(4,1)}), s8[2097152]{0:T(1024)(128)(4,1)S(1)}, s32[]{:S(2)}) async-start(s8[6291456]{0:T(1024)(128)(4,1)} %bitcast.472), calls=%async_computation.30 | async-start | bytes 4194304
  66.7 21.0 %all-to-all-start.4 = ((bf16[8,576,128]{2,1,0:T(8,128)(2,1)}), bf16[8,576,128]{2,1,0:T(8,128)(2,1)S(1)}, u32[]{:S(2)}, u32[]{:S(2)}) async-start(bf16[8,576,128]{2,1,0:T(8,128)(2,1)} %bitcast.47), calls=%async_computation.4 | async-start | bytes 2359296 | tf_op jit(solution)/shard_map/all_to_all | solution.py:63
  70.5 5.6 %copy-start.24 = (f32[8,36,768]{2,1,0:T(8,128)S(1)}, f32[8,36,768]{2,1,0:T(8,128)}, u32[]{:S(2)}) copy-start(f32[8,36,768]{2,1,0:T(8,128)} %fusion.54) | copy-start | bytes 2654212
  70.5 10.2 %slice-start = ((s8[6291456]{0:T(1024)(128)(4,1)}), s8[4194304]{0:T(1024)(128)(4,1)S(1)}, s32[]{:S(2)}) async-start(s8[6291456]{0:T(1024)(128)(4,1)} %bitcast.404), calls=%async_computation.15 | async-start | bytes 8388608
  88.7 20.7 %all-to-all-start.2 = ((bf16[8,576,128]{2,1,0:T(8,128)(2,1)}), bf16[8,576,128]{2,1,0:T(8,128)(2,1)S(1)}, u32[]{:S(2)}, u32[]{:S(2)}) async-start(bf16[8,576,128]{2,1,0:T(8,128)(2,1)} %bitcast.35), calls=%async_computation.2 | async-start | bytes 2359296 | tf_op jit(solution)/shard_map/all_to_all | solution.py:63
  92.3 5.6 %copy-start.25 = (f32[8,36,768]{2,1,0:T(8,128)S(1)}, f32[8,36,768]{2,1,0:T(8,128)}, u32[]{:S(2)}) copy-start(f32[8,36,768]{2,1,0:T(8,128)} %fusion.54) | copy-start | bytes 2654212
  92.3 10.1 %slice-start.2 = ((s8[6291456]{0:T(1024)(128)(4,1)}), s8[4194304]{0:T(1024)(128)(4,1)S(1)}, s32[]{:S(2)}) async-start(s8[6291456]{0:T(1024)(128)(4,1)} %bitcast.407), calls=%async_computation.17 | async-start | bytes 8388608
  109.5 20.7 %all-to-all-start.5 = ((bf16[8,576,128]{2,1,0:T(8,128)(2,1)}), bf16[8,576,128]{2,1,0:T(8,128)(2,1)S(1)}, u32[]{:S(2)}, u32[]{:S(2)}) async-start(bf16[8,576,128]{2,1,0:T(8,128)(2,1)} %bitcast.440), calls=%async_computation.5 | async-start | bytes 2359296 | tf_op jit(solution)/shard_map/all_to_all | solution.py:63
  130.2 45.8 %all-to-all-start.3 = ((bf16[8,1152,128]{2,1,0:T(8,128)(2,1)}), bf16[8,1152,128]{2,1,0:T(8,128)(2,1)}, u32[]{:S(2)}, u32[]{:S(2)}) async-start(bf16[8,1152,128]{2,1,0:T(8,128)(2,1)} %bitcast.437), calls=%async_computation.3 | async-start | bytes 4718592 | tf_op jit(solution)/shard_map/all_to_all | solution.py:63
  138.5 37.5 %collective-permute-start = (bf16[128,32,128]{2,0,1:T(8,128)(2,1)S(1)}, bf16[128,32,128]{2,0,1:T(8,128)(2,1)S(1)}, u32[]{:S(2)}, u32[]{:S(2)}) collective-permute-start(bf16[128,32,128]{2,0,1:T(8,128)(2,1)S(1)} %fusion.26), channel_id=1, source_target_pairs={{0,120},{8,0},{16,8},{24,16},{32,24},{40,32},{48,40},{56,48},{64,5... | collective-permute-start | bytes 3145736 | tf_op jit(solution)/shard_map/ppermute | solution.py:9
  178.4 21.8 %all-to-all-start.6 = ((bf16[8,576,128]{2,1,0:T(8,128)(2,1)}), bf16[8,576,128]{2,1,0:T(8,128)(2,1)}, u32[]{:S(2)}, u32[]{:S(2)}) async-start(bf16[8,576,128]{2,1,0:T(8,128)(2,1)} %bitcast.443), calls=%async_computation.6 | async-start | bytes 2359296 | tf_op jit(solution)/shard_map/all_to_all | solution.py:63
  200.2 21.0 %all-to-all-start.9 = ((bf16[8,576,128]{2,1,0:T(8,128)(2,1)}), bf16[8,576,128]{2,1,0:T(8,128)(2,1)S(1)}, u32[]{:S(2)}, u32[]{:S(2)}) async-start(bf16[8,576,128]{2,1,0:T(8,128)(2,1)} %bitcast.97), calls=%async_computation.9 | async-start | bytes 2359296 | tf_op jit(solution)/shard_map/all_to_all | solution.py:63
  204.0 10.2 %slice-start.4 = ((s8[6291456]{0:T(1024)(128)(4,1)}), s8[4194304]{0:T(1024)(128)(4,1)S(1)}, s32[]{:S(2)}) async-start(s8[6291456]{0:T(1024)(128)(4,1)} %bitcast.410), calls=%async_computation.19 | async-start | bytes 8388608
  222.2 20.8 %all-to-all-start.7 = ((bf16[8,576,128]{2,1,0:T(8,128)(2,1)}), bf16[8,576,128]{2,1,0:T(8,128)(2,1)S(1)}, u32[]{:S(2)}, u32[]{:S(2)}) async-start(bf16[8,576,128]{2,1,0:T(8,128)(2,1)} %bitcast.84), calls=%async_computation.7 | async-start | bytes 2359296 | tf_op jit(solution)/shard_map/all_to_all | solution.py:63
  225.8 5.6 %copy-start.21 = (f32[8,36,768]{2,1,0:T(8,128)S(1)}, f32[8,36,768]{2,1,0:T(8,128)}, u32[]{:S(2)}) copy-start(f32[8,36,768]{2,1,0:T(8,128)} %fusion.60) | copy-start | bytes 2654212
  225.8 10.1 %slice-start.6 = ((s8[6291456]{0:T(1024)(128)(4,1)}), s8[4194304]{0:T(1024)(128)(4,1)S(1)}, s32[]{:S(2)}) async-start(s8[6291456]{0:T(1024)(128)(4,1)} %bitcast.413), calls=%async_computation.21 | async-start | bytes 8388608
  243.0 20.7 %all-to-all-start.10 = ((bf16[8,576,128]{2,1,0:T(8,128)(2,1)}), bf16[8,576,128]{2,1,0:T(8,128)(2,1)S(1)}, u32[]{:S(2)}, u32[]{:S(2)}) async-start(bf16[8,576,128]{2,1,0:T(8,128)(2,1)} %bitcast.439), calls=%async_computation.10 | async-start | bytes 2359296 | tf_op jit(solution)/shard_map/all_to_all | solution.py:63
  263.7 42.8 %all-to-all-start.8 = ((bf16[8,1152,128]{2,1,0:T(8,128)(2,1)}), bf16[8,1152,128]{2,1,0:T(8,128)(2,1)}, u32[]{:S(2)}, u32[]{:S(2)}) async-start(bf16[8,1152,128]{2,1,0:T(8,128)(2,1)} %bitcast.438), calls=%async_computation.8 | async-start | bytes 4718592 | tf_op jit(solution)/shard_map/all_to_all | solution.py:63
  272.4 33.9 %collective-permute-start.1 = (bf16[128,32,128]{2,0,1:T(8,128)(2,1)S(1)}, bf16[128,32,128]{2,0,1:T(8,128)(2,1)S(1)}, u32[]{:S(2)}, u32[]{:S(2)}) collective-permute-start(bf16[128,32,128]{2,0,1:T(8,128)(2,1)S(1)} %fusion.25), channel_id=1, source_target_pairs={{0,120},{8,0},{16,8},{24,16},{32,24},{40,32},{48,40},{56,48},{64,5... | collective-permute-start | bytes 3145736 | tf_op jit(solution)/shard_map/ppermute | solution.py:9
  309.0 25.6 %all-to-all-start.13 = ((bf16[8,576,128]{2,1,0:T(8,128)(2,1)}), bf16[8,576,128]{2,1,0:T(8,128)(2,1)}, u32[]{:S(2)}, u32[]{:S(2)}) async-start(bf16[8,576,128]{2,1,0:T(8,128)(2,1)} %bitcast.444), calls=%async_computation.13 | async-start | bytes 2359296 | tf_op jit(solution)/shard_map/all_to_all | solution.py:63
  334.6 21.0 %all-to-all-start.11 = ((bf16[8,576,128]{2,1,0:T(8,128)(2,1)}), bf16[8,576,128]{2,1,0:T(8,128)(2,1)S(1)}, u32[]{:S(2)}, u32[]{:S(2)}) async-start(bf16[8,576,128]{2,1,0:T(8,128)(2,1)} %bitcast.124), calls=%async_computation.11 | async-start | bytes 2359296 | tf_op jit(solution)/shard_map/all_to_all | solution.py:63
  338.4 5.6 %copy-start.22 = (f32[8,36,768]{2,1,0:T(8,128)S(1)}, f32[8,36,768]{2,1,0:T(8,128)}, u32[]{:S(2)}) copy-start(f32[8,36,768]{2,1,0:T(8,128)} %fusion.66) | copy-start | bytes 2654212
  338.4 10.2 %slice-start.8 = ((s8[6291456]{0:T(1024)(128)(4,1)}), s8[4194304]{0:T(1024)(128)(4,1)S(1)}, s32[]{:S(2)}) async-start(s8[6291456]{0:T(1024)(128)(4,1)} %bitcast.416), calls=%async_computation.23 | async-start | bytes 8388608
  356.6 20.7 %all-to-all-start.14 = ((bf16[8,576,128]{2,1,0:T(8,128)(2,1)}), bf16[8,576,128]{2,1,0:T(8,128)(2,1)S(1)}, u32[]{:S(2)}, u32[]{:S(2)}) async-start(bf16[8,576,128]{2,1,0:T(8,128)(2,1)} %bitcast.156), calls=%async_computation.14 | async-start | bytes 2359296 | tf_op jit(solution)/shard_map/all_to_all | solution.py:63
  360.2 10.1 %slice-start.10 = ((s8[6291456]{0:T(1024)(128)(4,1)}), s8[4194304]{0:T(1024)(128)(4,1)S(1)}, s32[]{:S(2)}) async-start(s8[6291456]{0:T(1024)(128)(4,1)} %bitcast.419), calls=%async_computation.25 | async-start | bytes 8388608
  377.3 20.7 %all-to-all-start.12 = ((bf16[8,576,128]{2,1,0:T(8,128)(2,1)}), bf16[8,576,128]{2,1,0:T(8,128)(2,1)S(1)}, u32[]{:S(2)}, u32[]{:S(2)}) async-start(bf16[8,576,128]{2,1,0:T(8,128)(2,1)} %bitcast.441), calls=%async_computation.12 | async-start | bytes 2359296 | tf_op jit(solution)/shard_map/all_to_all | solution.py:63
  402.1 15.8 %collective-permute-start.2 = (bf16[128,32,128]{2,0,1:T(8,128)(2,1)S(1)}, bf16[128,32,128]{2,0,1:T(8,128)(2,1)S(1)}, u32[]{:S(2)}, u32[]{:S(2)}) collective-permute-start(bf16[128,32,128]{2,0,1:T(8,128)(2,1)S(1)} %fusion.24), channel_id=1, source_target_pairs={{0,120},{8,0},{16,8},{24,16},{32,24},{40,32},{48,40},{56,48},{64,5... | collective-permute-start | bytes 3145736 | tf_op jit(solution)/shard_map/ppermute | solution.py:9
  (28 other events, 72.1 us)
where the time goes:
time: 428 us; the launch traced here: 420 us
  waiting for transfers between devices  166 us (39%)
  matrix products  134 us (31%)
  starting transfers between devices  69.2 us (16%)
  local copies, waits for them, and re-layouts  45.5 us (11%)
  other arithmetic  4.93 us (1%)
    ppermute x3, waiting for transfers between devices, shifted(): lax.ppermute(x, axis, [(i, (i + by) % devices) for i in range(devices)])  84.5 us
    all_to_all x15, waiting for transfers between devices, exchange(): lax.all_to_all(flat, 'expert', split_axis=0, concat_axis=0, tiled=True)  81.2 us
    all_to_all x15, starting transfers between devices, exchange(): lax.all_to_all(flat, 'expert', split_axis=0, concat_axis=0, tiled=True)  66.5 us
    dot_general x6, matrix products, backward_part(): jnp.einsum('scjl,hjl->sch', grad_part, down_proj, preferred_element_type=...  33.4 us
    dot_general x6, matrix products, backward_part(): jnp.einsum('sch,jlh->scjl', grad_gate, gate_proj, preferred_element_type=...  27.2 us
    dot_general x3, matrix products, forward_part(): jnp.einsum('scjl,jlh->sch', input_part, up_proj, preferred_element_type=j...  21.6 us
    dot_general x3, matrix products, forward_part(): jnp.einsum('scjl,jlh->sch', input_part, gate_proj, preferred_element_type...  16 us
    dot_general x6, matrix products, backward_part(): jnp.einsum('sch,jlh->scjl', grad_up, up_proj, preferred_element_type=jnp....  13.3 us
  transfers between devices with their start and end apart: 18, of which 17 were waited for; matrix products, arithmetic and copies ran while one was open for 38% of the time, Pallas kernels for 0%

commit v1 on v0

--- a/solution.py
+++ b/solution.py
@@ -65,10 +65,12 @@
 
     plans = [route_plan(step) for step in range(rounds)]
     first_part = exchange(collect(plans[0][0], saved_inputs[0, 0].reshape(rows_dev, pieces, lanes)))
-    first_part, first_block, later_inputs, down_raw = lax.optimization_barrier(
-        (first_part, grad_in[0], saved_inputs[1:], w_down[0, 0])
+    first_part, first_block, later_inputs, down_raw, gate_raw, up_raw = lax.optimization_barrier(
+        (first_part, grad_in[0], saved_inputs[1:], w_down[0, 0], w_gate[0, 0], w_up[0, 0])
     )
     down_proj = down_raw.reshape(hidden, pieces, lanes)
+    gate_proj = gate_raw.reshape(pieces, lanes, hidden)
+    up_proj = up_raw.reshape(pieces, lanes, hidden)
     input_buffers = [None] + [
         collect(plans[step][0], later_inputs[step - 1, 0].reshape(rows_dev, pieces, lanes))
         for step in range(1, rounds)

time: 428 us -> 452 us (1.056)
  the two profiles are of different devices: /device:TPU:7 before, /device:TPU:1 now
where the time goes in v1:
time: 452 us; the launch traced here: 444 us
  waiting for transfers between devices  201 us (44%)
  matrix products  135 us (30%)
  starting transfers between devices  67.9 us (15%)
  local copies, waits for them, and re-layouts  36.5 us (8%)
    all_to_all x15, waiting for transfers between devices, exchange(): lax.all_to_all(flat, 'expert', split_axis=0, concat_axis=0, tiled=True)  116 us
    ppermute x3, waiting for transfers between devices, shifted(): lax.ppermute(x, axis, [(i, (i + by) % devices) for i in range(devices)])  84.7 us
    all_to_all x15, starting transfers between devices, exchange(): lax.all_to_all(flat, 'expert', split_axis=0, concat_axis=0, tiled=True)  65.2 us
    dot_general x6, matrix products, backward_part(): jnp.einsum('scjl,hjl->sch', grad_part, down_proj, preferred_element_type=...  34.4 us
    dot_general x6, matrix products, backward_part(): jnp.einsum('sch,jlh->scjl', grad_gate, gate_proj, preferred_element_type=...  28.1 us
    dot_general x3, matrix products, forward_part(): jnp.einsum('scjl,jlh->sch', input_part, gate_proj, preferred_element_type...  18.9 us
    dot_general x3, matrix products, forward_part(): jnp.einsum('scjl,jlh->sch', input_part, up_proj, preferred_element_type=j...  18.3 us
    dot_general x6, matrix products, backward_part(): jnp.einsum('sch,jlh->scjl', grad_up, up_proj, preferred_element_type=jnp....  13.3 us
  transfers between devices with their start and end apart: 18, of which 16 were waited for; matrix products, arithmetic and copies ran while one was open for 28% of the time, Pallas kernels for 0%

profile of v1, /device:TPU:1, one launch (start us, length us, event | category | flops | bytes accessed | tf_op | source)
XLA Modules:
  0.0 444.4 jit_solution(14681696735553260706)
XLA Ops:
  5.0 6.4 %all-to-all-start = ((bf16[8,1152,128]{2,1,0:T(8,128)(2,1)}), bf16[8,1152,128]{2,1,0:T(8,128)(2,1)}, u32[]{:S(2)}, u32[]{:S(2)}) async-start(bf16[8,1152,128]{2,1,0:T(8,128)(2,1)} %bitcast.11), calls=%async_computation | async-start | bytes 4718592 | tf_op jit(solution)/shard_map/all_to_all | solution.py:63
  16.9 24.5 %all-to-all-done = bf16[8,1152,128]{2,1,0:T(8,128)(2,1)} async-done(((bf16[8,1152,128]{2,1,0:T(8,128)(2,1)}), bf16[8,1152,128]{2,1,0:T(8,128)(2,1)}, u32[]{:S(2)}, u32[]{:S(2)}) %all-to-all-start) | async-done | bytes 2359328 | tf_op jit(solution)/shard_map/all_to_all | solution.py:63
  43.8 6.1 %all-to-all-start.4 = ((bf16[8,576,128]{2,1,0:T(8,128)(2,1)}), bf16[8,576,128]{2,1,0:T(8,128)(2,1)}, u32[]{:S(2)}, u32[]{:S(2)}) async-start(bf16[8,576,128]{2,1,0:T(8,128)(2,1)} %bitcast.450), calls=%async_computation.4 | async-start | bytes 2359296 | tf_op jit(solution)/shard_map/all_to_all | solution.py:63
  51.2 5.8 %fusion.57 = f32[8,36,768]{2,1,0:T(8,128)S(1)} fusion(bf16[32,128,768,1]{2,1,0,3:T(8,128)(2,1)} %bitcast.471, bf16[8,36,32,128]{3,2,1,0:T(8,128)(2,1)} %bitcast.12), kind=kOutput, calls=%fused_computation.83 | convolution fusion | flops 1811939328 | bytes 9535488 | tf_op jit(solution)/shard_map/scjl,jlh->sch/dot_general | solution.py:13
  57.1 10.2 %all-to-all-done.4 = bf16[8,576,128]{2,1,0:T(8,128)(2,1)} async-done(((bf16[8,576,128]{2,1,0:T(8,128)(2,1)}), bf16[8,576,128]{2,1,0:T(8,128)(2,1)}, u32[]{:S(2)}, u32[]{:S(2)}) %all-to-all-start.4) | async-done | bytes 1179680 | tf_op jit(solution)/shard_map/all_to_all | solution.py:63
  71.0 7.2 %fusion.54 = f32[8,36,768]{2,1,0:T(8,128)} fusion(bf16[32,128,768,1]{2,1,0,3:T(8,128)(2,1)} %bitcast.403, bf16[8,36,32,128]{3,2,1,0:T(8,128)(2,1)} %bitcast.12), kind=kOutput, calls=%fused_computation.82 | convolution fusion | flops 1811939328 | bytes 9535488 | tf_op jit(solution)/shard_map/scjl,jlh->sch/dot_general | solution.py:14
  79.5 6.3 %fusion.75 = f32[8,18,768]{2,1,0:T(8,128)} fusion(bf16[8,18,32,128]{3,2,1,0:T(8,128)(2,1)} %bitcast.50, bf16[768,4096]{1,0:T(8,128)(2,1)} %bitcast.465), kind=kOutput, calls=%fused_computation.89 | convolution fusion | flops 905969664 | bytes 7913472 | tf_op jit(solution)/shard_map/scjl,hjl->sch/dot_general | solution.py:19
  88.2 5.2 %fusion.72 = f32[8,18,768]{2,1,0:T(8,128)S(1)} fusion(bf16[8,18,32,128]{3,2,1,0:T(8,128)(2,1)S(1)} %bitcast.457, bf16[768,4096]{1,0:T(8,128)(2,1)} %bitcast.466), kind=kOutput, calls=%fused_computation.88 | convolution fusion | flops 905969664 | bytes 7913472 | tf_op jit(solution)/shard_map/scjl,hjl->sch/dot_general | solution.py:19
  93.4 4.6 %fusion.122 = f32[8,18,32,128]{3,1,2,0:T(8,128)S(1)} fusion(bf16[32,128,768,1]{2,1,0,3:T(8,128)(2,1)} %bitcast.472, f32[8,18,768]{2,1,0:T(8,128)S(1)} %fusion.72, f32[8,36,768]{2,1,0:T(8,128)S(1)} %copy-done.25, f32[8,36,768]{2,1,0:T(8,128)S(1)} %fusion.57), kind=kOutput, calls=%fused_computation.144 | convolution fusion | flops 907075584 | bytes 10420224 | tf_op jit(solution)/shard_map/sch,jlh->scjl/dot_general | solution.py:24
  105.3 4.9 %fusion.119 = f32[8,18,32,128]{3,1,2,0:T(8,128)S(1)} fusion(bf16[32,128,768,1]{2,1,0,3:T(8,128)(2,1)} %bitcast.473, f32[8,18,768]{2,1,0:T(8,128)} %fusion.75, f32[8,36,768]{2,1,0:T(8,128)} %fusion.54, f32[8,36,768]{2,1,0:T(8,128)} %copy-done.5), kind=kOutput, calls=%fused_computation.141 | convolution fusion | flops 907075584 | bytes 10420224 | tf_op jit(solution)/shard_map/sch,jlh->scjl/dot_general | solution.py:24
  113.8 8.6 %all-to-all-done.2 = bf16[8,576,128]{2,1,0:T(8,128)(2,1)S(1)} async-done(((bf16[8,576,128]{2,1,0:T(8,128)(2,1)}), bf16[8,576,128]{2,1,0:T(8,128)(2,1)S(1)}, u32[]{:S(2)}, u32[]{:S(2)}) %all-to-all-start.2) | async-done | bytes 1179680 | tf_op jit(solution)/shard_map/all_to_all | solution.py:63
  131.9 11.7 %all-to-all-done.5 = bf16[8,576,128]{2,1,0:T(8,128)(2,1)S(1)} async-done(((bf16[8,576,128]{2,1,0:T(8,128)(2,1)}), bf16[8,576,128]{2,1,0:T(8,128)(2,1)S(1)}, u32[]{:S(2)}, u32[]{:S(2)}) %all-to-all-start.5) | async-done | bytes 1179680 | tf_op jit(solution)/shard_map/all_to_all | solution.py:63
  152.3 36.7 %collective-permute-done = bf16[128,32,128]{2,0,1:T(8,128)(2,1)S(1)} collective-permute-done((bf16[128,32,128]{2,0,1:T(8,128)(2,1)S(1)}, bf16[128,32,128]{2,0,1:T(8,128)(2,1)S(1)}, u32[]{:S(2)}, u32[]{:S(2)}) %collective-permute-start) | collective-permute-done | bytes 1048608 | tf_op jit(solution)/shard_map/ppermute | solution.py:9
  197.1 5.8 %fusion.63 = f32[8,36,768]{2,1,0:T(8,128)S(1)} fusion(bf16[32,128,768,1]{2,1,0,3:T(8,128)(2,1)} %bitcast.474, bf16[8,36,32,128]{3,2,1,0:T(8,128)(2,1)} %bitcast.43), kind=kOutput, calls=%fused_computation.85 | convolution fusion | flops 1811939328 | bytes 9535488 | tf_op jit(solution)/shard_map/scjl,jlh->sch/dot_general | solution.py:13
  202.9 10.5 %all-to-all-done.9 = bf16[8,576,128]{2,1,0:T(8,128)(2,1)} async-done(((bf16[8,576,128]{2,1,0:T(8,128)(2,1)}), bf16[8,576,128]{2,1,0:T(8,128)(2,1)}, u32[]{:S(2)}, u32[]{:S(2)}) %all-to-all-start.9) | async-done | bytes 1179680 | tf_op jit(solution)/shard_map/all_to_all | solution.py:63
  217.5 5.9 %fusion.60 = f32[8,36,768]{2,1,0:T(8,128)S(1)} fusion(bf16[32,128,768,1]{2,1,0,3:T(8,128)(2,1)} %bitcast.404, bf16[8,36,32,128]{3,2,1,0:T(8,128)(2,1)} %bitcast.43), kind=kOutput, calls=%fused_computation.84 | convolution fusion | flops 1811939328 | bytes 9535488 | tf_op jit(solution)/shard_map/scjl,jlh->sch/dot_general | solution.py:14
  223.3 6.6 %fusion.81 = f32[8,18,768]{2,1,0:T(8,128)} fusion(bf16[8,18,32,128]{3,2,1,0:T(8,128)(2,1)} %bitcast.100, bf16[768,4096]{1,0:T(8,128)(2,1)} %bitcast.467), kind=kOutput, calls=%fused_computation.91 | convolution fusion | flops 905969664 | bytes 7913472 | tf_op jit(solution)/shard_map/scjl,hjl->sch/dot_general | solution.py:19
  229.9 4.8 %all-to-all-done.6 = bf16[8,576,128]{2,1,0:T(8,128)(2,1)S(1)} async-done(((bf16[8,576,128]{2,1,0:T(8,128)(2,1)}), bf16[8,576,128]{2,1,0:T(8,128)(2,1)S(1)}, u32[]{:S(2)}, u32[]{:S(2)}) %all-to-all-start.6) | async-done | bytes 1179680 | tf_op jit(solution)/shard_map/all_to_all | solution.py:63
  234.7 5.2 %fusion.78 = f32[8,18,768]{2,1,0:T(8,128)S(1)} fusion(bf16[8,18,32,128]{3,2,1,0:T(8,128)(2,1)S(1)} %bitcast.458, bf16[768,4096]{1,0:T(8,128)(2,1)} %bitcast.468), kind=kOutput, calls=%fused_computation.90 | convolution fusion | flops 905969664 | bytes 7913472 | tf_op jit(solution)/shard_map/scjl,hjl->sch/dot_general | solution.py:19
  251.6 4.9 %fusion.113 = f32[8,18,32,128]{3,1,2,0:T(8,128)S(1)} fusion(bf16[32,128,768,1]{2,1,0,3:T(8,128)(2,1)} %bitcast.476, f32[8,18,768]{2,1,0:T(8,128)} %fusion.81, f32[8,36,768]{2,1,0:T(8,128)} %copy-done.26, f32[8,36,768]{2,1,0:T(8,128)} %copy-done.8), kind=kOutput, calls=%fused_computation.135 | convolution fusion | flops 907075584 | bytes 10420224 | tf_op jit(solution)/shard_map/sch,jlh->scjl/dot_general | solution.py:24
  260.2 8.6 %all-to-all-done.7 = bf16[8,576,128]{2,1,0:T(8,128)(2,1)S(1)} async-done(((bf16[8,576,128]{2,1,0:T(8,128)(2,1)}), bf16[8,576,128]{2,1,0:T(8,128)(2,1)S(1)}, u32[]{:S(2)}, u32[]{:S(2)}) %all-to-all-start.7) | async-done | bytes 1179680 | tf_op jit(solution)/shard_map/all_to_all | solution.py:63
  276.5 13.0 %all-to-all-done.10 = bf16[8,576,128]{2,1,0:T(8,128)(2,1)S(1)} async-done(((bf16[8,576,128]{2,1,0:T(8,128)(2,1)}), bf16[8,576,128]{2,1,0:T(8,128)(2,1)S(1)}, u32[]{:S(2)}, u32[]{:S(2)}) %all-to-all-start.10) | async-done | bytes 1179680 | tf_op jit(solution)/shard_map/all_to_all | solution.py:63
  289.5 4.6 %all-to-all-start.8 = ((bf16[8,1152,128]{2,1,0:T(8,128)(2,1)}), bf16[8,1152,128]{2,1,0:T(8,128)(2,1)}, u32[]{:S(2)}, u32[]{:S(2)}) async-start(bf16[8,1152,128]{2,1,0:T(8,128)(2,1)} %bitcast.442), calls=%async_computation.8 | async-start | bytes 4718592 | tf_op jit(solution)/shard_map/all_to_all | solution.py:63
  298.4 33.2 %collective-permute-done.1 = bf16[128,32,128]{2,0,1:T(8,128)(2,1)S(1)} collective-permute-done((bf16[128,32,128]{2,0,1:T(8,128)(2,1)S(1)}, bf16[128,32,128]{2,0,1:T(8,128)(2,1)S(1)}, u32[]{:S(2)}, u32[]{:S(2)}) %collective-permute-start.1) | collective-permute-done | bytes 1048608 | tf_op jit(solution)/shard_map/ppermute | solution.py:9
  335.2 5.8 %all-to-all-start.11 = ((bf16[8,576,128]{2,1,0:T(8,128)(2,1)}), bf16[8,576,128]{2,1,0:T(8,128)(2,1)}, u32[]{:S(2)}, u32[]{:S(2)}) async-start(bf16[8,576,128]{2,1,0:T(8,128)(2,1)} %bitcast.449), calls=%async_computation.11 | async-start | bytes 2359296 | tf_op jit(solution)/shard_map/all_to_all | solution.py:63
  341.0 7.3 %fusion.69 = f32[8,36,768]{2,1,0:T(8,128)} fusion(bf16[32,128,768,1]{2,1,0,3:T(8,128)(2,1)} %bitcast.477, bf16[8,36,32,128]{3,2,1,0:T(8,128)(2,1)} %bitcast.94), kind=kOutput, calls=%fused_computation.87 | convolution fusion | flops 1811939328 | bytes 9535488 | tf_op jit(solution)/shard_map/scjl,jlh->sch/dot_general | solution.py:13
  349.6 5.2 %fusion.66 = f32[8,36,768]{2,1,0:T(8,128)} fusion(bf16[32,128,768,1]{2,1,0,3:T(8,128)(2,1)S(1)} %bitcast.419, bf16[8,36,32,128]{3,2,1,0:T(8,128)(2,1)} %bitcast.94), kind=kOutput, calls=%fused_computation.86 | convolution fusion | flops 1811939328 | bytes 9535488 | tf_op jit(solution)/shard_map/scjl,jlh->sch/dot_general | solution.py:14
  362.2 5.6 %fusion.84 = f32[8,18,768]{2,1,0:T(8,128)S(1)} fusion(bf16[8,18,32,128]{3,2,1,0:T(8,128)(2,1)} %bitcast.127, bf16[768,4096]{1,0:T(8,128)(2,1)} %bitcast.469), kind=kOutput, calls=%fused_computation.92 | convolution fusion | flops 905969664 | bytes 7913472 | tf_op jit(solution)/shard_map/scjl,hjl->sch/dot_general | solution.py:19
  384.0 5.6 %fusion.87 = f32[8,18,768]{2,1,0:T(8,128)S(1)} fusion(bf16[8,18,32,128]{3,2,1,0:T(8,128)(2,1)} %bitcast.456, bf16[768,4096]{1,0:T(8,128)(2,1)} %bitcast.470), kind=kOutput, calls=%fused_computation.93 | convolution fusion | flops 905969664 | bytes 7913472 | tf_op jit(solution)/shard_map/scjl,hjl->sch/dot_general | solution.py:19
  389.6 4.6 %fusion.107 = f32[8,18,32,128]{3,1,2,0:T(8,128)S(1)} fusion(bf16[32,128,768,1]{2,1,0,3:T(8,128)(2,1)} %bitcast.479, f32[8,18,768]{2,1,0:T(8,128)S(1)} %fusion.87, f32[8,36,768]{2,1,0:T(8,128)S(1)} %copy-done.24, f32[8,36,768]{2,1,0:T(8,128)S(1)} %copy-done.7), kind=kOutput, calls=%fused_computation.129 | convolution fusion | flops 907075584 | bytes 10420224 | tf_op jit(solution)/shard_map/sch,jlh->scjl/dot_general | solution.py:24
  410.2 11.7 %all-to-all-done.14 = bf16[8,576,128]{2,1,0:T(8,128)(2,1)S(1)} async-done(((bf16[8,576,128]{2,1,0:T(8,128)(2,1)}), bf16[8,576,128]{2,1,0:T(8,128)(2,1)S(1)}, u32[]{:S(2)}, u32[]{:S(2)}) %all-to-all-start.14) | async-done | bytes 1179680 | tf_op jit(solution)/shard_map/all_to_all | solution.py:63
  427.1 14.9 %collective-permute-done.2 = bf16[128,32,128]{2,0,1:T(8,128)(2,1)S(1)} collective-permute-done((bf16[128,32,128]{2,0,1:T(8,128)(2,1)S(1)}, bf16[128,32,128]{2,0,1:T(8,128)(2,1)S(1)}, u32[]{:S(2)}, u32[]{:S(2)}) %collective-permute-start.2) | collective-permute-done | bytes 1048608 | tf_op jit(solution)/shard_map/ppermute | solution.py:9
  (182 shorter events, 141.2 us)
Async XLA Ops:
  0.9 15.9 %copy-start.18 = (s32[128,2]{0,1:T(2,128)}, s32[128,2]{0,1:T(2,128)S(1)}, u32[]{:S(2)}) copy-start(s32[128,2]{0,1:T(2,128)S(1)} %get-tuple-element.42) | copy-start | bytes 3076
  5.0 36.3 %all-to-all-start = ((bf16[8,1152,128]{2,1,0:T(8,128)(2,1)}), bf16[8,1152,128]{2,1,0:T(8,128)(2,1)}, u32[]{:S(2)}, u32[]{:S(2)}) async-start(bf16[8,1152,128]{2,1,0:T(8,128)(2,1)} %bitcast.11), calls=%async_computation | async-start | bytes 4718592 | tf_op jit(solution)/shard_map/all_to_all | solution.py:63
  43.8 23.4 %all-to-all-start.4 = ((bf16[8,576,128]{2,1,0:T(8,128)(2,1)}), bf16[8,576,128]{2,1,0:T(8,128)(2,1)}, u32[]{:S(2)}, u32[]{:S(2)}) async-start(bf16[8,576,128]{2,1,0:T(8,128)(2,1)} %bitcast.450), calls=%async_computation.4 | async-start | bytes 2359296 | tf_op jit(solution)/shard_map/all_to_all | solution.py:63
  57.1 41.0 %copy-start.5 = (f32[8,36,768]{2,1,0:T(8,128)}, f32[8,36,768]{2,1,0:T(8,128)S(1)}, u32[]{:S(2)}) copy-start(f32[8,36,768]{2,1,0:T(8,128)S(1)} %fusion.57) | copy-start | bytes 2654212
  67.2 21.0 %all-to-all-start.1 = ((bf16[8,576,128]{2,1,0:T(8,128)(2,1)}), bf16[8,576,128]{2,1,0:T(8,128)(2,1)S(1)}, u32[]{:S(2)}, u32[]{:S(2)}) async-start(bf16[8,576,128]{2,1,0:T(8,128)(2,1)} %bitcast.19), calls=%async_computation.1 | async-start | bytes 2359296 | tf_op jit(solution)/shard_map/all_to_all | solution.py:63
  88.2 9.8 %slice-start = ((s8[6291456]{0:T(1024)(128)(4,1)}), s8[4194304]{0:T(1024)(128)(4,1)S(1)}, s32[]{:S(2)}) async-start(s8[6291456]{0:T(1024)(128)(4,1)} %bitcast.405), calls=%async_computation.15 | async-start | bytes 8388608
  101.5 20.9 %all-to-all-start.2 = ((bf16[8,576,128]{2,1,0:T(8,128)(2,1)}), bf16[8,576,128]{2,1,0:T(8,128)(2,1)S(1)}, u32[]{:S(2)}, u32[]{:S(2)}) async-start(bf16[8,576,128]{2,1,0:T(8,128)(2,1)} %bitcast.447), calls=%async_computation.2 | async-start | bytes 2359296 | tf_op jit(solution)/shard_map/all_to_all | solution.py:63
  122.4 21.2 %all-to-all-start.5 = ((bf16[8,576,128]{2,1,0:T(8,128)(2,1)}), bf16[8,576,128]{2,1,0:T(8,128)(2,1)S(1)}, u32[]{:S(2)}, u32[]{:S(2)}) async-start(bf16[8,576,128]{2,1,0:T(8,128)(2,1)} %bitcast.446), calls=%async_computation.5 | async-start | bytes 2359296 | tf_op jit(solution)/shard_map/all_to_all | solution.py:63
  143.6 45.3 %all-to-all-start.3 = ((bf16[8,1152,128]{2,1,0:T(8,128)(2,1)}), bf16[8,1152,128]{2,1,0:T(8,128)(2,1)}, u32[]{:S(2)}, u32[]{:S(2)}) async-start(bf16[8,1152,128]{2,1,0:T(8,128)(2,1)} %bitcast.441), calls=%async_computation.3 | async-start | bytes 4718592 | tf_op jit(solution)/shard_map/all_to_all | solution.py:63
  151.4 37.6 %collective-permute-start = (bf16[128,32,128]{2,0,1:T(8,128)(2,1)S(1)}, bf16[128,32,128]{2,0,1:T(8,128)(2,1)S(1)}, u32[]{:S(2)}, u32[]{:S(2)}) collective-permute-start(bf16[128,32,128]{2,0,1:T(8,128)(2,1)S(1)} %fusion.26), channel_id=1, source_target_pairs={{0,120},{8,0},{16,8},{24,16},{32,24},{40,32},{48,40},{56,48},{64,5... | collective-permute-start | bytes 3145736 | tf_op jit(solution)/shard_map/ppermute | solution.py:9
  191.4 22.1 %all-to-all-start.9 = ((bf16[8,576,128]{2,1,0:T(8,128)(2,1)}), bf16[8,576,128]{2,1,0:T(8,128)(2,1)}, u32[]{:S(2)}, u32[]{:S(2)}) async-start(bf16[8,576,128]{2,1,0:T(8,128)(2,1)} %bitcast.451), calls=%async_computation.9 | async-start | bytes 2359296 | tf_op jit(solution)/shard_map/all_to_all | solution.py:63
  202.9 41.6 %copy-start.8 = (f32[8,36,768]{2,1,0:T(8,128)}, f32[8,36,768]{2,1,0:T(8,128)S(1)}, u32[]{:S(2)}) copy-start(f32[8,36,768]{2,1,0:T(8,128)S(1)} %fusion.63) | copy-start | bytes 2654212
  213.5 21.2 %all-to-all-start.6 = ((bf16[8,576,128]{2,1,0:T(8,128)(2,1)}), bf16[8,576,128]{2,1,0:T(8,128)(2,1)S(1)}, u32[]{:S(2)}, u32[]{:S(2)}) async-start(bf16[8,576,128]{2,1,0:T(8,128)(2,1)} %bitcast.73), calls=%async_computation.6 | async-start | bytes 2359296 | tf_op jit(solution)/shard_map/all_to_all | solution.py:63
  223.3 16.6 %copy-start.26 = (f32[8,36,768]{2,1,0:T(8,128)}, f32[8,36,768]{2,1,0:T(8,128)S(1)}, u32[]{:S(2)}) copy-start(f32[8,36,768]{2,1,0:T(8,128)S(1)} %fusion.60) | copy-start | bytes 2654212
  246.7 9.8 %slice-start.6 = ((s8[6291456]{0:T(1024)(128)(4,1)}), s8[2097152]{0:T(1024)(128)(4,1)S(1)}, s32[]{:S(2)}) async-start(s8[6291456]{0:T(1024)(128)(4,1)} %bitcast.414), calls=%async_computation.21 | async-start | bytes 4194304
  248.0 20.8 %all-to-all-start.7 = ((bf16[8,576,128]{2,1,0:T(8,128)(2,1)}), bf16[8,576,128]{2,1,0:T(8,128)(2,1)S(1)}, u32[]{:S(2)}, u32[]{:S(2)}) async-start(bf16[8,576,128]{2,1,0:T(8,128)(2,1)} %bitcast.448), calls=%async_computation.7 | async-start | bytes 2359296 | tf_op jit(solution)/shard_map/all_to_all | solution.py:63
  258.9 13.5 %copy-start.17 = (s32[128,2]{0,1:T(2,128)S(1)}, s32[128,2]{0,1:T(2,128)}, u32[]{:S(2)}) copy-start(s32[128,2]{0,1:T(2,128)} %copy-done.16) | copy-start | bytes 3076
  258.9 13.5 %copy-start.19 = (s32[128,2]{0,1:T(2,128)S(1)}, s32[128,2]{0,1:T(2,128)}, u32[]{:S(2)}) copy-start(s32[128,2]{0,1:T(2,128)} %copy-done.18) | copy-start | bytes 3076
  258.9 13.5 %copy-start.20 = (f32[128,2]{0,1:T(2,128)S(1)}, f32[128,2]{0,1:T(2,128)}, u32[]{:S(2)}) copy-start(f32[128,2]{0,1:T(2,128)} %get-tuple-element.44) | copy-start | bytes 3076
  258.9 13.5 %copy-start.21 = (f32[128,2]{0,1:T(2,128)S(1)}, f32[128,2]{0,1:T(2,128)}, u32[]{:S(2)}) copy-start(f32[128,2]{0,1:T(2,128)} %get-tuple-element.46) | copy-start | bytes 3076
  258.9 13.5 %copy-start.15 = (pred[128,288]{0,1:T(8,128)(4,1)S(1)}, pred[128,288]{0,1:T(8,128)(4,1)}, u32[]{:S(2)}) copy-start(pred[128,288]{0,1:T(8,128)(4,1)} %get-tuple-element.49) | copy-start | bytes 110596
  268.8 20.7 %all-to-all-start.10 = ((bf16[8,576,128]{2,1,0:T(8,128)(2,1)}), bf16[8,576,128]{2,1,0:T(8,128)(2,1)S(1)}, u32[]{:S(2)}, u32[]{:S(2)}) async-start(bf16[8,576,128]{2,1,0:T(8,128)(2,1)} %bitcast.443), calls=%async_computation.10 | async-start | bytes 2359296 | tf_op jit(solution)/shard_map/all_to_all | solution.py:63
  289.5 42.1 %all-to-all-start.8 = ((bf16[8,1152,128]{2,1,0:T(8,128)(2,1)}), bf16[8,1152,128]{2,1,0:T(8,128)(2,1)}, u32[]{:S(2)}, u32[]{:S(2)}) async-start(bf16[8,1152,128]{2,1,0:T(8,128)(2,1)} %bitcast.442), calls=%async_computation.8 | async-start | bytes 4718592 | tf_op jit(solution)/shard_map/all_to_all | solution.py:63
  297.5 34.1 %collective-permute-start.1 = (bf16[128,32,128]{2,0,1:T(8,128)(2,1)S(1)}, bf16[128,32,128]{2,0,1:T(8,128)(2,1)S(1)}, u32[]{:S(2)}, u32[]{:S(2)}) collective-permute-start(bf16[128,32,128]{2,0,1:T(8,128)(2,1)S(1)} %fusion.25), channel_id=1, source_target_pairs={{0,120},{8,0},{16,8},{24,16},{32,24},{40,32},{48,40},{56,48},{64,5... | collective-permute-start | bytes 3145736 | tf_op jit(solution)/shard_map/ppermute | solution.py:9
  333.9 15.7 %slice-start.8 = ((s8[6291456]{0:T(1024)(128)(4,1)}), s8[2097152]{0:T(1024)(128)(4,1)S(1)}, s32[]{:S(2)}) async-start(s8[6291456]{0:T(1024)(128)(4,1)} %bitcast.417), calls=%async_computation.23 | async-start | bytes 4194304
  335.2 23.2 %all-to-all-start.11 = ((bf16[8,576,128]{2,1,0:T(8,128)(2,1)}), bf16[8,576,128]{2,1,0:T(8,128)(2,1)}, u32[]{:S(2)}, u32[]{:S(2)}) async-start(bf16[8,576,128]{2,1,0:T(8,128)(2,1)} %bitcast.449), calls=%async_computation.11 | async-start | bytes 2359296 | tf_op jit(solution)/shard_map/all_to_all | solution.py:63
  358.3 21.0 %all-to-all-start.13 = ((bf16[8,576,128]{2,1,0:T(8,128)(2,1)}), bf16[8,576,128]{2,1,0:T(8,128)(2,1)S(1)}, u32[]{:S(2)}, u32[]{:S(2)}) async-start(bf16[8,576,128]{2,1,0:T(8,128)(2,1)} %bitcast.445), calls=%async_computation.13 | async-start | bytes 2359296 | tf_op jit(solution)/shard_map/all_to_all | solution.py:63
  362.2 10.1 %slice-start.10 = ((s8[6291456]{0:T(1024)(128)(4,1)}), s8[4194304]{0:T(1024)(128)(4,1)S(1)}, s32[]{:S(2)}) async-start(s8[6291456]{0:T(1024)(128)(4,1)} %bitcast.420), calls=%async_computation.25 | async-start | bytes 8388608
  380.4 20.8 %all-to-all-start.12 = ((bf16[8,576,128]{2,1,0:T(8,128)(2,1)}), bf16[8,576,128]{2,1,0:T(8,128)(2,1)S(1)}, u32[]{:S(2)}, u32[]{:S(2)}) async-start(bf16[8,576,128]{2,1,0:T(8,128)(2,1)} %bitcast.139), calls=%async_computation.12 | async-start | bytes 2359296 | tf_op jit(solution)/shard_map/all_to_all | solution.py:63
  384.0 10.2 %slice-start.12 = ((s8[6291456]{0:T(1024)(128)(4,1)}), s8[4194304]{0:T(1024)(128)(4,1)S(1)}, s32[]{:S(2)}) async-start(s8[6291456]{0:T(1024)(128)(4,1)} %bitcast.423), calls=%async_computation.27 | async-start | bytes 8388608
  401.1 20.7 %all-to-all-start.14 = ((bf16[8,576,128]{2,1,0:T(8,128)(2,1)}), bf16[8,576,128]{2,1,0:T(8,128)(2,1)S(1)}, u32[]{:S(2)}, u32[]{:S(2)}) async-start(bf16[8,576,128]{2,1,0:T(8,128)(2,1)} %bitcast.444), calls=%async_computation.14 | async-start | bytes 2359296 | tf_op jit(solution)/shard_map/all_to_all | solution.py:63
  426.2 15.8 %collective-permute-start.2 = (bf16[128,32,128]{2,0,1:T(8,128)(2,1)S(1)}, bf16[128,32,128]{2,0,1:T(8,128)(2,1)S(1)}, u32[]{:S(2)}, u32[]{:S(2)}) collective-permute-start(bf16[128,32,128]{2,0,1:T(8,128)(2,1)S(1)} %fusion.24), channel_id=1, source_target_pairs={{0,120},{8,0},{16,8},{24,16},{32,24},{40,32},{48,40},{56,48},{64,5... | collective-permute-start | bytes 3145736 | tf_op jit(solution)/shard_map/ppermute | solution.py:9
  (29 other events, 124.0 us)
